TPU v7x, 256 devices: a whole 4x4x8 slice. The times are simulated.
256 devices in a mesh: dp: 32 (over z_lo, y, x), tensor: 8 (over z_hi, core).
Axes of the slice: x: 4, y: 4, z: 8 (z_hi: 4, z_lo: 2; z = z_hi * 2 + z_lo), core: 2. Of those that a mesh axis runs over, the one named last changes fastest.
Arguments:
- embeds: bfloat16 [512, 4608], P('dp'), may hold values from -6 to 6
- owner: int32 [64, 8], P('dp'), may hold values from 0 to 7, each once within a row
- pairs: int32 [64, 56, 2], P('dp'), may hold values from 0 to 7, as said below
- pref_weight: bfloat16 [2, 4608, 4608], P(None, 'dp', 'tensor'), may hold values from -0.0625 to 0.0625
- pref_bias: float32 [4608], P('tensor'), may hold values from -3 to 3
- pref_out: float32 [4608], P('tensor'), may hold values from -0.375 to 0.375
- logratio: float32 [512], P('dp'), may hold values from -3 to 3
- attn_out: bfloat16 [32768, 4096], P('dp', 'tensor'), may hold values from -6 to 6
- grad_out: bfloat16 [32768, 4608], P('dp', 'tensor'), may hold values from -6 to 6
- w_out: bfloat16 [4608, 4096], P('dp', 'tensor'), may hold values from -0.09375 to 0.09375
Outputs:
- d_attn: bfloat16 [32768, 4096], P('dp', 'tensor')
- o_grad: float32 [4608, 4096], P('dp', 'tensor')
Inputs may be any that keep to these rules, and one draw needn't show every extreme that they name: `pairs`: the two numbers of a pair differ. Each row of owner names every number once.
All inputs are finite; a program needn't handle non-finite values.
Results may differ from a plain program's by a relative error of at most 0.0049.
Values may be sent and summed in bfloat16 or wider, within the bound.
No kernel may reach another device: no remote copies, remote signals or barrier semaphores. Data moves between devices by JAX's collectives and lax.ppermute only.
A program may use at most 128 MiB of HBM per device.

v0:
```python
import jax
import jax.numpy as jnp
from jax import lax
from jax.sharding import Mesh
from jax.sharding import PartitionSpec as P

eta_scale = 2.0
DP = ("zl", "y", "x")
TP = ("zh", "c")
PLANE = ("y", "x")


def shards(
    embeds, owner, pairs, pref_weight, pref_bias, pref_out, logratio, attn_out, grad_out, w_out
):
    resp_dev = embeds.shape[0]
    prompts_dev = owner.shape[0]
    groups = owner.shape[1]
    npairs = pairs.shape[1]
    width_local = pref_weight.shape[2]
    rows_w = pref_weight.shape[1]
    n_dp = lax.axis_size(DP)
    n_zl = lax.axis_size("zl")
    n_plane = lax.axis_size(PLANE)
    zl = lax.axis_index("zl")
    swap = [(k, (k + 1) % n_zl) for k in range(n_zl)]
    features = lax.all_gather(grad_out, TP, axis=1, tiled=True)
    w_other = lax.ppermute(w_out, "zl", swap)
    other = lax.ppermute(pref_weight, "zl", swap)
    w_pair = jnp.where(zl == 0, jnp.stack([w_out, w_other]), jnp.stack([w_other, w_out]))
    copies = jnp.broadcast_to(w_pair[None], (n_plane,) + w_pair.shape)
    piece = lax.all_to_all(copies, PLANE, 0, 0, tiled=True)
    piece = piece.transpose(1, 0, 2, 3).reshape(-1, w_out.shape[1])
    pair_w = jnp.where(
        zl == 0,
        jnp.concatenate([pref_weight, other], axis=1),
        jnp.concatenate([other, pref_weight], axis=1),
    )
    cols = embeds.reshape(resp_dev, n_zl, n_plane, rows_w).transpose(2, 0, 1, 3)
    cols = cols.reshape(n_plane, resp_dev * n_zl * rows_w // 128, 128)
    cols = lax.all_to_all(cols, PLANE, 0, 0, tiled=True).reshape(n_plane * resp_dev, n_zl * rows_w)
    part = jnp.concatenate(
        [
            jnp.dot(cols, pair_w[0], preferred_element_type=jnp.float32),
            jnp.dot(cols, pair_w[1], preferred_element_type=jnp.float32),
        ],
        axis=1,
    )
    part = part.reshape(n_plane, resp_dev, part.shape[1])
    proj = jnp.sum(lax.all_to_all(part, PLANE, 0, 0, tiled=True), axis=0)
    base = (jnp.arange(prompts_dev, dtype=jnp.int32) * groups)[:, None]
    row_a = base + jnp.take_along_axis(owner, pairs[:, :, 0], axis=1)
    row_b = base + jnp.take_along_axis(owner, pairs[:, :, 1], axis=1)
    upper = proj[:, :width_local][row_a.reshape(-1)]
    lower = proj[:, width_local:][row_b.reshape(-1)]
    pre = (upper + lower).reshape(prompts_dev, npairs, width_local)
    hidden = jax.nn.gelu(pre + pref_bias)
    partial_logit = jnp.sum(hidden * pref_out, axis=-1)
    logit = lax.psum(partial_logit, TP)
    prob = jax.nn.sigmoid(logit)
    numbers = jnp.arange(groups, dtype=jnp.int32)
    first = (pairs[:, :, 0][:, :, None] == numbers).astype(jnp.float32)
    second = (pairs[:, :, 1][:, :, None] == numbers).astype(jnp.float32)
    wins = jnp.sum(prob[:, :, None] * first + (1.0 - prob)[:, :, None] * second, axis=1)
    count = jnp.sum(first + second, axis=1)
    winrate = (wins + 1.0) / (count + 2.0)
    placed = (owner[:, :, None] == numbers).astype(jnp.float32)
    rowrate = jnp.sum(winrate[:, :, None] * placed, axis=1).reshape(-1)
    coef = 2.0 * (logratio - eta_scale * (rowrate - 0.5))
    weighted = (
        (
            features.astype(jnp.float32).reshape(resp_dev, -1, features.shape[1])
            * coef[:, None, None]
        )
        .reshape(features.shape)
        .astype(jnp.bfloat16)
    )
    total_resp = resp_dev * n_dp
    full = lax.dot_general(
        weighted, attn_out, (((0,), (0,)), ((), ())), preferred_element_type=jnp.float32
    )
    full = full.astype(jnp.bfloat16).reshape(n_zl, n_plane, -1, full.shape[1])
    first_half = jnp.where(zl == 0, full[1], full[0])
    own_half = jnp.where(zl == 0, full[0], full[1])
    theirs = jnp.sum(
        lax.all_to_all(first_half, PLANE, 0, 0, tiled=True).astype(jnp.float32), axis=0
    )
    got = lax.ppermute(theirs, "zl", swap)
    shares = lax.all_to_all(own_half, PLANE, 0, 0, tiled=True)
    d_attn = jnp.dot(weighted, piece, preferred_element_type=jnp.float32).astype(jnp.bfloat16)
    shares, d_attn = lax.optimization_barrier((shares, d_attn))
    mine = jnp.sum(shares.astype(jnp.float32), axis=0)
    o_grad = (mine + got) / total_resp
    return (d_attn, o_grad)


def solution(mesh):
    n_zl = 2
    fine = Mesh(
        mesh.devices.reshape(n_zl, mesh.shape["dp"] // (n_zl * 4), 4, mesh.shape["tensor"] // 2, 2),
        ("zl", "y", "x", "zh", "c"),
    )
    return jax.shard_map(
        shards,
        mesh=fine,
        in_specs=(
            P(DP, None),
            P(DP, None),
            P(DP, None, None),
            P(None, DP, TP),
            P(TP),
            P(TP),
            P(DP),
            P(DP, TP),
            P(DP, TP),
            P(DP, TP),
        ),
        out_specs=(P(DP, TP), P(DP, TP)),
        check_vma=False,
    )
```

profile of v0, /device:TPU:64, one launch (start us, length us, event | category | flops | bytes accessed | tf_op | source)
XLA Modules:
  0.0 200.9 jit_solution(1344475992000351544)
XLA Ops:
  7.9 2.0 collective-permute-start
  9.9 1.3 reshape.160
  11.5 1.1 reshape.161
  12.6 7.0 %all-to-all-start = ((bf16[16,36,128]{2,1,0:T(8,128)(2,1)}), bf16[16,36,128]{2,1,0:T(8,128)(2,1)S(1)}, u32[]{:S(2)}, u32[]{:S(2)}) async-start(bf16[16,36,128]{2,1,0:T(8,128)(2,1)} %reshape.161), calls=%async_computation | async-start | bytes 327680 | tf_op jit(solution)/shard_map/all_to_all | solution.py:41
  20.6 7.2 %all-to-all-done = bf16[16,36,128]{2,1,0:T(8,128)(2,1)S(1)} async-done(((bf16[16,36,128]{2,1,0:T(8,128)(2,1)}), bf16[16,36,128]{2,1,0:T(8,128)(2,1)S(1)}, u32[]{:S(2)}, u32[]{:S(2)}) %all-to-all-start) | async-done | bytes 147488 | tf_op jit(solution)/shard_map/all_to_all | solution.py:41
  28.1 1.3 maximum_select_fusion
  30.2 1.4 copy.18
  31.6 3.7 %all-to-all-start.1 = ((f32[16,16,1152]{2,1,0:T(8,128)}), f32[16,16,1152]{2,1,0:T(8,128)S(1)}, u32[]{:S(2)}, u32[]{:S(2)}) async-start(f32[16,16,1152]{2,1,0:T(8,128)} %bitcast.6), calls=%async_computation.1 | async-start | bytes 2359296 | tf_op jit(solution)/shard_map/all_to_all | solution.py:50
  35.4 2.0 %gather_fusion.2 = s32[112]{0:T(128)S(1)} fusion(s32[2,8]{1,0:T(2,128)S(1)} %copy-done.1, s32[112]{0:T(128)S(1)} %reshape.207), kind=kCustom, calls=%fused_computation.clone | custom fusion | bytes 1792 | tf_op jit(solution)/shard_map/jit(take_along_axis)/gather | solution.py:52
  37.6 2.0 %gather_fusion.3 = s32[112]{0:T(128)S(1)} fusion(s32[2,8]{1,0:T(2,128)S(1)} %copy-done.1, s32[112]{0:T(128)S(1)} %reshape.212), kind=kCustom, calls=%fused_computation.1.clone | custom fusion | bytes 1792 | tf_op jit(solution)/shard_map/jit(take_along_axis)/gather | solution.py:53
  40.0 13.0 %all-to-all-done.1 = f32[16,16,1152]{2,1,0:T(8,128)S(1)} async-done(((f32[16,16,1152]{2,1,0:T(8,128)}), f32[16,16,1152]{2,1,0:T(8,128)S(1)}, u32[]{:S(2)}, u32[]{:S(2)}) %all-to-all-start.1) | async-done | bytes 1179680 | tf_op jit(solution)/shard_map/all_to_all | solution.py:50
  53.0 2.6 %broadcast_in_dim.4 = bf16[16,2,144,512]{3,2,1,0:T(8,128)(2,1)} broadcast(bf16[2,144,512]{2,1,0:T(8,128)(2,1)S(1)} %maximum_select_fusion.1), dimensions={1,2,3} | broadcast | bytes 5013504 | tf_op jit(solution)/shard_map/broadcast_in_dim | solution.py:31
  55.7 4.6 %all-to-all-start.3 = ((bf16[16,2,144,512]{3,2,1,0:T(8,128)(2,1)}), bf16[16,2,144,512]{3,2,1,0:T(8,128)(2,1)}, u32[]{:S(2)}, u32[]{:S(2)}) async-start(bf16[16,2,144,512]{3,2,1,0:T(8,128)(2,1)} %broadcast_in_dim.4), calls=%async_computation.3 | async-start | bytes 9437184 | tf_op jit(solution)/shard_map/all_to_all | solution.py:32
  62.3 16.0 %psum.7 = f32[2,56]{1,0:T(2,128)S(1)} all-reduce(f32[2,56]{1,0:T(2,128)S(1)} %reduce_sum.67), channel_id=1, replica_groups=mesh['zl'=2,'y'=4,'x'=4,'zh'=4,'c'=2] {'zh','c'}, use_global_device_ids=true, to_apply=%region_2.4 | all-reduce | flops 112 | bytes 896 | tf_op jit(solution)/shard_map/psum | solution.py:59
  78.8 29.8 %all-gather.2.cloned.1.call-done = bf16[1024,4608]{0,1:T(8,128)(2,1)} async-done(((bf16[1024,576]{0,1:T(8,128)(2,1)}), bf16[1024,4608]{0,1:T(8,128)(2,1)}) %all-gather.2.cloned.1.call-update) | async-done | bytes 9437200 | tf_op jit(solution)/shard_map/all_gather | solution.py:27
  108.6 9.0 %fusion.2 = bf16[4608,512]{1,0:T(8,128)(2,1)S(1)} fusion(bf16[1024,512]{1,0:T(8,128)(2,1)S(1)} %copy-done, bf16[1024,4608]{0,1:T(8,128)(2,1)} %all-gather.2.cloned.1.call-done, f32[1024]{0:T(1024)S(1)} %mul.109), kind=kOutput, calls=%fused_computation.7 | convolution fusion | flops 4848353280 | bytes 15208448 | tf_op jit(solution)/shard_map/dot_general | solution.py:79
  117.6 1.7 broadcast_select_fusion
  119.3 6.6 %all-to-all-done.3 = bf16[16,2,144,512]{3,2,1,0:T(8,128)(2,1)} async-done(((bf16[16,2,144,512]{3,2,1,0:T(8,128)(2,1)}), bf16[16,2,144,512]{3,2,1,0:T(8,128)(2,1)}, u32[]{:S(2)}, u32[]{:S(2)}) %all-to-all-start.3) | async-done | bytes 4718624 | tf_op jit(solution)/shard_map/all_to_all | solution.py:32
  125.9 32.7 %all_to_all.25 = bf16[16,144,512]{2,1,0:T(8,128)(2,1)} all-to-all(bf16[16,144,512]{2,1,0:T(8,128)(2,1)S(1)} %bitcast.40), channel_id=1, replica_groups=mesh['zl'=2,'y'=4,'x'=4,'zh'=4,'c'=2] {'y','x'}, dimensions={0} | all-to-all | bytes 4718592 | tf_op jit(solution)/shard_map/all_to_all | solution.py:86
  158.6 3.7 %all-to-all-start.2 = ((bf16[16,144,512]{2,1,0:T(8,128)(2,1)}), bf16[16,144,512]{2,1,0:T(8,128)(2,1)S(1)}, u32[]{:S(2)}, u32[]{:S(2)}) async-start(bf16[16,144,512]{2,1,0:T(8,128)(2,1)} %bitcast.39), calls=%async_computation.2 | async-start | bytes 4718592 | tf_op jit(solution)/shard_map/all_to_all | solution.py:89
  162.4 2.8 %copy.19 = bf16[16,2,144,512]{3,2,0,1:T(8,128)(2,1)S(1)} copy(bf16[16,2,144,512]{3,2,1,0:T(8,128)(2,1)} %all-to-all-done.3) | data formatting | bytes 9437184 | tf_op jit(solution)/shard_map/all_to_all | solution.py:32
  166.8 8.8 %fusion.3 = bf16[1024,512]{1,0:T(8,128)(2,1)} fusion(bf16[4608,512]{1,0:T(8,128)(2,1)S(1)} %bitcast.41, bf16[1024,4608]{0,1:T(8,128)(2,1)} %all-gather.2.cloned.1.call-done, f32[1024]{0:T(1024)S(1)} %mul.109), kind=kOutput, calls=%fused_computation.12 | convolution fusion | flops 4846518272 | bytes 15208448 | tf_op jit(solution)/shard_map/dot_general | solution.py:90
  175.6 16.3 %all-to-all-done.2 = bf16[16,144,512]{2,1,0:T(8,128)(2,1)S(1)} async-done(((bf16[16,144,512]{2,1,0:T(8,128)(2,1)}), bf16[16,144,512]{2,1,0:T(8,128)(2,1)S(1)}, u32[]{:S(2)}, u32[]{:S(2)}) %all-to-all-start.2) | async-done | bytes 2359328 | tf_op jit(solution)/shard_map/all_to_all | solution.py:89
  192.3 1.7 add_multiply_fusion
  (59 shorter events, 8.1 us)
Async XLA Ops:
  7.2 101.4 %copy-start = (bf16[1024,512]{1,0:T(8,128)(2,1)S(1)}, bf16[1024,512]{1,0:T(8,128)(2,1)}, u32[]{:S(2)}) copy-start(bf16[1024,512]{1,0:T(8,128)(2,1)} %param.19) | copy-start | bytes 3145732
  7.2 101.4 %all-gather.2.cloned.1.call-start = ((), (), s32[]{:S(2)}) async-start(), calls=%async_computation.5 | async-start | bytes 10616832 | tf_op jit(solution)/shard_map/all_gather | solution.py:27
  7.9 20.2 %collective-permute-start = (bf16[2,144,576]{2,1,0:T(8,128)(2,1)}, bf16[2,144,576]{2,1,0:T(8,128)(2,1)S(1)}, u32[]{:S(2)}, u32[]{:S(2)}) collective-permute-start(bf16[2,144,576]{2,1,0:T(8,128)(2,1)} %param.15), channel_id=1, source_target_pairs={{0,128},{128,0},{1,129},{129,1},{2,130},{130,2},{3,131},{131,3},{4... | collective-permute-start | bytes 995336 | tf_op jit(solution)/shard_map/ppermute | solution.py:29
  12.6 15.2 %all-to-all-start = ((bf16[16,36,128]{2,1,0:T(8,128)(2,1)}), bf16[16,36,128]{2,1,0:T(8,128)(2,1)S(1)}, u32[]{:S(2)}, u32[]{:S(2)}) async-start(bf16[16,36,128]{2,1,0:T(8,128)(2,1)} %reshape.161), calls=%async_computation | async-start | bytes 327680 | tf_op jit(solution)/shard_map/all_to_all | solution.py:41
  19.6 20.3 %collective-permute-start.1 = (bf16[144,512]{1,0:T(8,128)(2,1)}, bf16[144,512]{1,0:T(8,128)(2,1)S(1)}, u32[]{:S(2)}, u32[]{:S(2)}) collective-permute-start(bf16[144,512]{1,0:T(8,128)(2,1)} %param.21), channel_id=1, source_target_pairs={{0,128},{128,0},{1,129},{129,1},{2,130},{130,2},{3,131},{131,3},{4... | collective-permute-start | bytes 442376 | tf_op jit(solution)/shard_map/ppermute | solution.py:28
  29.4 6.0 %copy-start.1 = (s32[2,8]{1,0:T(2,128)S(1)}, s32[2,8]{1,0:T(2,128)}, u32[]{:S(2)}) copy-start(s32[2,8]{1,0:T(2,128)} %param.13) | copy-start | bytes 196
  30.1 9.8 %copy-start.3 = (bf16[144,512]{1,0:T(8,128)(2,1)S(1)}, bf16[144,512]{1,0:T(8,128)(2,1)}, u32[]{:S(2)}) copy-start(bf16[144,512]{1,0:T(8,128)(2,1)} %param.21) | copy-start | bytes 442372
  31.6 21.4 %all-to-all-start.1 = ((f32[16,16,1152]{2,1,0:T(8,128)}), f32[16,16,1152]{2,1,0:T(8,128)S(1)}, u32[]{:S(2)}, u32[]{:S(2)}) async-start(f32[16,16,1152]{2,1,0:T(8,128)} %bitcast.6), calls=%async_computation.1 | async-start | bytes 2359296 | tf_op jit(solution)/shard_map/all_to_all | solution.py:50
  55.7 70.3 %all-to-all-start.3 = ((bf16[16,2,144,512]{3,2,1,0:T(8,128)(2,1)}), bf16[16,2,144,512]{3,2,1,0:T(8,128)(2,1)}, u32[]{:S(2)}, u32[]{:S(2)}) async-start(bf16[16,2,144,512]{3,2,1,0:T(8,128)(2,1)} %broadcast_in_dim.4), calls=%async_computation.3 | async-start | bytes 9437184 | tf_op jit(solution)/shard_map/all_to_all | solution.py:32
  60.2 1.8 copy-start.4
  60.2 1.8 copy-start.5
  60.2 18.4 %copy-start.6 = (f32[16]{0:T(128)S(1)}, f32[16]{0:T(128)}, u32[]{:S(2)}) copy-start(f32[16]{0:T(128)} %param.18) | copy-start | bytes 196
  158.6 33.3 %all-to-all-start.2 = ((bf16[16,144,512]{2,1,0:T(8,128)(2,1)}), bf16[16,144,512]{2,1,0:T(8,128)(2,1)S(1)}, u32[]{:S(2)}, u32[]{:S(2)}) async-start(bf16[16,144,512]{2,1,0:T(8,128)(2,1)} %bitcast.39), calls=%async_computation.2 | async-start | bytes 4718592 | tf_op jit(solution)/shard_map/all_to_all | solution.py:89
  162.4 3.1 %copy-start.2 = (bf16[16,144,512]{2,1,0:T(8,128)(2,1)S(1)}, bf16[16,144,512]{2,1,0:T(8,128)(2,1)}, u32[]{:S(2)}) copy-start(bf16[16,144,512]{2,1,0:T(8,128)(2,1)} %all_to_all.25) | copy-start | bytes 7077892
  166.5 25.8 %collective-permute-start.2 = (f32[144,512]{1,0:T(8,128)}, f32[144,512]{1,0:T(8,128)}, u32[]{:S(2)}, u32[]{:S(2)}) collective-permute-start(f32[144,512]{1,0:T(8,128)} %convert_reduce_fusion), channel_id=1, source_target_pairs={{0,128},{128,0},{1,129},{129,1},{2,130},{130,2},{3,131},{131,3},{4... | collective-permute-start | bytes 884744 | tf_op jit(solution)/shard_map/ppermute | solution.py:88
Sparse Core Ops, SparseCore 0:
  9.8 98.6 all-gather.1
where the time goes:
time: 201 us
  waiting for transfers between devices  73.7 us (37%)
  blocking collectives  48.7 us (24%)
  starting transfers between devices  21.5 us (11%)
  matrix products  18.6 us (9%)
  local copies, waits for them, and re-layouts  17.3 us (9%)
  between operations  14.3 us (7%)
  other arithmetic  6.84 us (3%)
    all_to_all x1, blocking collectives, shards(): lax.all_to_all(first_half, PLANE, 0, 0, tiled=True).astype(jnp.float32)  32.7 us
    all_gather x1, waiting for transfers between devices, shards(): features = lax.all_gather(grad_out, TP, axis=1, tiled=True)  29.8 us
    all_to_all x1, waiting for transfers between devices, shards(): shares = lax.all_to_all(own_half, PLANE, 0, 0, tiled=True)  16.3 us
    psum x1, blocking collectives, shards(): logit = lax.psum(partial_logit, TP)  16 us
    all_to_all x1, waiting for transfers between devices, shards(): proj = jnp.sum(lax.all_to_all(part, PLANE, 0, 0, tiled=True), axis=0)  13 us
    dot_general x1, matrix products, shards(): lax.dot_general(weighted, attn_out, (((0,), (0,)), ((), ())), preferred_e...  9.03 us
    dot_general x1, matrix products, shards(): jnp.dot(weighted, piece, preferred_element_type=jnp.float32)  8.83 us
    all_to_all x1, waiting for transfers between devices, shards(): lax.all_to_all(cols, PLANE, 0, 0, tiled=True)  7.21 us
  transfers between devices with their start and end apart: 8, of which 5 were waited for; matrix products, arithmetic and copies ran while one was open for 20% of the time, Pallas kernels for 0%

commit v1 on v0

--- a/solution.py
+++ b/solution.py
@@ -56,7 +56,7 @@
     pre = (upper + lower).reshape(prompts_dev, npairs, width_local)
     hidden = jax.nn.gelu(pre + pref_bias)
     partial_logit = jnp.sum(hidden * pref_out, axis=-1)
-    logit = lax.psum(partial_logit, TP)
+    logit = jnp.sum(lax.all_gather(partial_logit, axis_name=TP), 0)
     prob = jax.nn.sigmoid(logit)
     numbers = jnp.arange(groups, dtype=jnp.int32)
     first = (pairs[:, :, 0][:, :, None] == numbers).astype(jnp.float32)

time: 201 us -> 201 us (level)
  blocking collectives: 48.7 us -> 44.8 us
  waiting for transfers between devices: 73.7 us -> 77.4 us
    psum x1 -> x0, blocking collectives: 16 us -> none  [shards(): logit = lax.psum(partial_logit, TP)]
    all_gather x0 -> x1, blocking collectives: none -> 12.1 us  [shards(): logit = jnp.sum(lax.all_gather(partial_logit, axis_name=TP), 0)]
    all_gather x1, waiting for transfers between devices: 29.8 us -> 33.5 us  [shards(): features = lax.all_gather(grad_out, TP, axis=1, tiled=True)]
where the time goes in v1:
time: 201 us
  waiting for transfers between devices  77.4 us (39%)
  blocking collectives  44.8 us (22%)
  starting transfers between devices  21.7 us (11%)
  matrix products  18.6 us (9%)
  local copies, waits for them, and re-layouts  17.3 us (9%)
  between operations  14.3 us (7%)
  other arithmetic  6.86 us (3%)
    all_gather x1, waiting for transfers between devices, shards(): features = lax.all_gather(grad_out, TP, axis=1, tiled=True)  33.5 us
    all_to_all x1, blocking collectives, shards(): lax.all_to_all(first_half, PLANE, 0, 0, tiled=True).astype(jnp.float32)  32.7 us
    all_to_all x1, waiting for transfers between devices, shards(): shares = lax.all_to_all(own_half, PLANE, 0, 0, tiled=True)  16.2 us
    all_to_all x1, waiting for transfers between devices, shards(): proj = jnp.sum(lax.all_to_all(part, PLANE, 0, 0, tiled=True), axis=0)  13 us
    all_gather x1, blocking collectives, shards(): logit = jnp.sum(lax.all_gather(partial_logit, axis_name=TP), 0)  12.1 us
    dot_general x1, matrix products, shards(): lax.dot_general(weighted, attn_out, (((0,), (0,)), ((), ())), preferred_e...  9.03 us
    dot_general x1, matrix products, shards(): jnp.dot(weighted, piece, preferred_element_type=jnp.float32)  8.83 us
    all_to_all x1, waiting for transfers between devices, shards(): lax.all_to_all(cols, PLANE, 0, 0, tiled=True)  7.21 us
  transfers between devices with their start and end apart: 8, of which 5 were waited for; matrix products, arithmetic and copies ran while one was open for 20% of the time, Pallas kernels for 0%

profile of v1, /device:TPU:64, one launch (start us, length us, event | category | flops | bytes accessed | tf_op | source)
XLA Modules:
  0.0 200.9 jit_solution(349256657537173928)
XLA Ops:
  7.9 2.0 collective-permute-start
  9.9 1.3 reshape.168
  11.5 1.1 reshape.169
  12.6 7.0 %all-to-all-start = ((bf16[16,36,128]{2,1,0:T(8,128)(2,1)}), bf16[16,36,128]{2,1,0:T(8,128)(2,1)S(1)}, u32[]{:S(2)}, u32[]{:S(2)}) async-start(bf16[16,36,128]{2,1,0:T(8,128)(2,1)} %reshape.169), calls=%async_computation | async-start | bytes 327680 | tf_op jit(solution)/shard_map/all_to_all | solution.py:41
  20.6 7.2 %all-to-all-done = bf16[16,36,128]{2,1,0:T(8,128)(2,1)S(1)} async-done(((bf16[16,36,128]{2,1,0:T(8,128)(2,1)}), bf16[16,36,128]{2,1,0:T(8,128)(2,1)S(1)}, u32[]{:S(2)}, u32[]{:S(2)}) %all-to-all-start) | async-done | bytes 147488 | tf_op jit(solution)/shard_map/all_to_all | solution.py:41
  28.1 1.3 maximum_select_fusion
  30.2 1.4 copy.18
  31.6 3.7 %all-to-all-start.1 = ((f32[16,16,1152]{2,1,0:T(8,128)}), f32[16,16,1152]{2,1,0:T(8,128)S(1)}, u32[]{:S(2)}, u32[]{:S(2)}) async-start(f32[16,16,1152]{2,1,0:T(8,128)} %bitcast.6), calls=%async_computation.1 | async-start | bytes 2359296 | tf_op jit(solution)/shard_map/all_to_all | solution.py:50
  35.4 2.0 %gather_fusion.2 = s32[112]{0:T(128)S(1)} fusion(s32[2,8]{1,0:T(2,128)S(1)} %copy-done.1, s32[112]{0:T(128)S(1)} %reshape.215), kind=kCustom, calls=%fused_computation.clone | custom fusion | bytes 1792 | tf_op jit(solution)/shard_map/jit(take_along_axis)/gather | solution.py:52
  37.6 2.0 %gather_fusion.3 = s32[112]{0:T(128)S(1)} fusion(s32[2,8]{1,0:T(2,128)S(1)} %copy-done.1, s32[112]{0:T(128)S(1)} %reshape.220), kind=kCustom, calls=%fused_computation.1.clone | custom fusion | bytes 1792 | tf_op jit(solution)/shard_map/jit(take_along_axis)/gather | solution.py:53
  40.0 13.0 %all-to-all-done.1 = f32[16,16,1152]{2,1,0:T(8,128)S(1)} async-done(((f32[16,16,1152]{2,1,0:T(8,128)}), f32[16,16,1152]{2,1,0:T(8,128)S(1)}, u32[]{:S(2)}, u32[]{:S(2)}) %all-to-all-start.1) | async-done | bytes 1179680 | tf_op jit(solution)/shard_map/all_to_all | solution.py:50
  53.0 2.6 %broadcast_in_dim.4 = bf16[16,2,144,512]{3,2,1,0:T(8,128)(2,1)} broadcast(bf16[2,144,512]{2,1,0:T(8,128)(2,1)S(1)} %maximum_select_fusion.1), dimensions={1,2,3} | broadcast | bytes 5013504 | tf_op jit(solution)/shard_map/broadcast_in_dim | solution.py:31
  55.7 4.6 %all-to-all-start.3 = ((bf16[16,2,144,512]{3,2,1,0:T(8,128)(2,1)}), bf16[16,2,144,512]{3,2,1,0:T(8,128)(2,1)}, u32[]{:S(2)}, u32[]{:S(2)}) async-start(bf16[16,2,144,512]{3,2,1,0:T(8,128)(2,1)} %broadcast_in_dim.4), calls=%async_computation.3 | async-start | bytes 9437184 | tf_op jit(solution)/shard_map/all_to_all | solution.py:32
  62.3 12.1 %all_gather.11 = f32[8,2,56]{2,1,0:T(2,128)S(1)} all-gather(f32[1,2,56]{2,1,0:T(2,128)S(1)} %all_gather.10), channel_id=1, replica_groups=mesh['zl'=2,'y'=4,'x'=4,'zh'=4,'c'=2] {'zh','c'}, dimensions={0}, use_global_device_ids=true | all-gather | bytes 4032 | tf_op jit(solution)/shard_map/all_gather | solution.py:59
  74.9 33.5 %all-gather.2.cloned.1.call-done = bf16[1024,4608]{0,1:T(8,128)(2,1)} async-done(((bf16[1024,576]{0,1:T(8,128)(2,1)}), bf16[1024,4608]{0,1:T(8,128)(2,1)}) %all-gather.2.cloned.1.call-update) | async-done | bytes 9437200 | tf_op jit(solution)/shard_map/all_gather | solution.py:27
  108.4 9.0 %fusion.2 = bf16[4608,512]{1,0:T(8,128)(2,1)S(1)} fusion(bf16[1024,512]{1,0:T(8,128)(2,1)S(1)} %copy-done, bf16[1024,4608]{0,1:T(8,128)(2,1)} %all-gather.2.cloned.1.call-done, f32[1024]{0:T(1024)S(1)} %mul.109), kind=kOutput, calls=%fused_computation.7 | convolution fusion | flops 4848353280 | bytes 15208448 | tf_op jit(solution)/shard_map/dot_general | solution.py:79
  117.4 1.7 broadcast_select_fusion
  119.1 6.8 %all-to-all-done.3 = bf16[16,2,144,512]{3,2,1,0:T(8,128)(2,1)} async-done(((bf16[16,2,144,512]{3,2,1,0:T(8,128)(2,1)}), bf16[16,2,144,512]{3,2,1,0:T(8,128)(2,1)}, u32[]{:S(2)}, u32[]{:S(2)}) %all-to-all-start.3) | async-done | bytes 4718624 | tf_op jit(solution)/shard_map/all_to_all | solution.py:32
  125.9 32.7 %all_to_all.25 = bf16[16,144,512]{2,1,0:T(8,128)(2,1)} all-to-all(bf16[16,144,512]{2,1,0:T(8,128)(2,1)S(1)} %bitcast.40), channel_id=1, replica_groups=mesh['zl'=2,'y'=4,'x'=4,'zh'=4,'c'=2] {'y','x'}, dimensions={0} | all-to-all | bytes 4718592 | tf_op jit(solution)/shard_map/all_to_all | solution.py:86
  158.6 3.9 %all-to-all-start.2 = ((bf16[16,144,512]{2,1,0:T(8,128)(2,1)}), bf16[16,144,512]{2,1,0:T(8,128)(2,1)S(1)}, u32[]{:S(2)}, u32[]{:S(2)}) async-start(bf16[16,144,512]{2,1,0:T(8,128)(2,1)} %bitcast.39), calls=%async_computation.2 | async-start | bytes 4718592 | tf_op jit(solution)/shard_map/all_to_all | solution.py:89
  162.6 2.8 %copy.19 = bf16[16,2,144,512]{3,2,0,1:T(8,128)(2,1)S(1)} copy(bf16[16,2,144,512]{3,2,1,0:T(8,128)(2,1)} %all-to-all-done.3) | data formatting | bytes 9437184 | tf_op jit(solution)/shard_map/all_to_all | solution.py:32
  167.0 8.8 %fusion.3 = bf16[1024,512]{1,0:T(8,128)(2,1)} fusion(bf16[4608,512]{1,0:T(8,128)(2,1)S(1)} %bitcast.41, bf16[1024,4608]{0,1:T(8,128)(2,1)} %all-gather.2.cloned.1.call-done, f32[1024]{0:T(1024)S(1)} %mul.109), kind=kOutput, calls=%fused_computation.12 | convolution fusion | flops 4846518272 | bytes 15208448 | tf_op jit(solution)/shard_map/dot_general | solution.py:90
  175.8 16.2 %all-to-all-done.2 = bf16[16,144,512]{2,1,0:T(8,128)(2,1)S(1)} async-done(((bf16[16,144,512]{2,1,0:T(8,128)(2,1)}), bf16[16,144,512]{2,1,0:T(8,128)(2,1)S(1)}, u32[]{:S(2)}, u32[]{:S(2)}) %all-to-all-start.2) | async-done | bytes 2359328 | tf_op jit(solution)/shard_map/all_to_all | solution.py:89
  192.3 1.7 add_multiply_fusion
  (60 shorter events, 8.1 us)
Async XLA Ops:
  7.2 101.2 %copy-start = (bf16[1024,512]{1,0:T(8,128)(2,1)S(1)}, bf16[1024,512]{1,0:T(8,128)(2,1)}, u32[]{:S(2)}) copy-start(bf16[1024,512]{1,0:T(8,128)(2,1)} %param.19) | copy-start | bytes 3145732
  7.2 101.2 %all-gather.2.cloned.1.call-start = ((), (), s32[]{:S(2)}) async-start(), calls=%async_computation.5 | async-start | bytes 10616832 | tf_op jit(solution)/shard_map/all_gather | solution.py:27
  7.9 20.2 %collective-permute-start = (bf16[2,144,576]{2,1,0:T(8,128)(2,1)}, bf16[2,144,576]{2,1,0:T(8,128)(2,1)S(1)}, u32[]{:S(2)}, u32[]{:S(2)}) collective-permute-start(bf16[2,144,576]{2,1,0:T(8,128)(2,1)} %param.15), channel_id=1, source_target_pairs={{0,128},{128,0},{1,129},{129,1},{2,130},{130,2},{3,131},{131,3},{4... | collective-permute-start | bytes 995336 | tf_op jit(solution)/shard_map/ppermute | solution.py:29
  12.6 15.2 %all-to-all-start = ((bf16[16,36,128]{2,1,0:T(8,128)(2,1)}), bf16[16,36,128]{2,1,0:T(8,128)(2,1)S(1)}, u32[]{:S(2)}, u32[]{:S(2)}) async-start(bf16[16,36,128]{2,1,0:T(8,128)(2,1)} %reshape.169), calls=%async_computation | async-start | bytes 327680 | tf_op jit(solution)/shard_map/all_to_all | solution.py:41
  19.6 20.3 %collective-permute-start.1 = (bf16[144,512]{1,0:T(8,128)(2,1)}, bf16[144,512]{1,0:T(8,128)(2,1)S(1)}, u32[]{:S(2)}, u32[]{:S(2)}) collective-permute-start(bf16[144,512]{1,0:T(8,128)(2,1)} %param.21), channel_id=1, source_target_pairs={{0,128},{128,0},{1,129},{129,1},{2,130},{130,2},{3,131},{131,3},{4... | collective-permute-start | bytes 442376 | tf_op jit(solution)/shard_map/ppermute | solution.py:28
  29.4 6.0 %copy-start.1 = (s32[2,8]{1,0:T(2,128)S(1)}, s32[2,8]{1,0:T(2,128)}, u32[]{:S(2)}) copy-start(s32[2,8]{1,0:T(2,128)} %param.13) | copy-start | bytes 196
  30.1 9.8 %copy-start.3 = (bf16[144,512]{1,0:T(8,128)(2,1)S(1)}, bf16[144,512]{1,0:T(8,128)(2,1)}, u32[]{:S(2)}) copy-start(bf16[144,512]{1,0:T(8,128)(2,1)} %param.21) | copy-start | bytes 442372
  31.6 21.4 %all-to-all-start.1 = ((f32[16,16,1152]{2,1,0:T(8,128)}), f32[16,16,1152]{2,1,0:T(8,128)S(1)}, u32[]{:S(2)}, u32[]{:S(2)}) async-start(f32[16,16,1152]{2,1,0:T(8,128)} %bitcast.6), calls=%async_computation.1 | async-start | bytes 2359296 | tf_op jit(solution)/shard_map/all_to_all | solution.py:50
  55.7 70.3 %all-to-all-start.3 = ((bf16[16,2,144,512]{3,2,1,0:T(8,128)(2,1)}), bf16[16,2,144,512]{3,2,1,0:T(8,128)(2,1)}, u32[]{:S(2)}, u32[]{:S(2)}) async-start(bf16[16,2,144,512]{3,2,1,0:T(8,128)(2,1)} %broadcast_in_dim.4), calls=%async_computation.3 | async-start | bytes 9437184 | tf_op jit(solution)/shard_map/all_to_all | solution.py:32
  60.2 1.8 copy-start.4
  60.2 1.8 copy-start.5
  60.2 14.5 %copy-start.6 = (f32[16]{0:T(128)S(1)}, f32[16]{0:T(128)}, u32[]{:S(2)}) copy-start(f32[16]{0:T(128)} %param.18) | copy-start | bytes 196
  158.6 33.3 %all-to-all-start.2 = ((bf16[16,144,512]{2,1,0:T(8,128)(2,1)}), bf16[16,144,512]{2,1,0:T(8,128)(2,1)S(1)}, u32[]{:S(2)}, u32[]{:S(2)}) async-start(bf16[16,144,512]{2,1,0:T(8,128)(2,1)} %bitcast.39), calls=%async_computation.2 | async-start | bytes 4718592 | tf_op jit(solution)/shard_map/all_to_all | solution.py:89
  162.6 3.1 %copy-start.2 = (bf16[16,144,512]{2,1,0:T(8,128)(2,1)S(1)}, bf16[16,144,512]{2,1,0:T(8,128)(2,1)}, u32[]{:S(2)}) copy-start(bf16[16,144,512]{2,1,0:T(8,128)(2,1)} %all_to_all.25) | copy-start | bytes 7077892
  166.7 25.6 %collective-permute-start.2 = (f32[144,512]{1,0:T(8,128)}, f32[144,512]{1,0:T(8,128)}, u32[]{:S(2)}, u32[]{:S(2)}) collective-permute-start(f32[144,512]{1,0:T(8,128)} %convert_reduce_fusion), channel_id=1, source_target_pairs={{0,128},{128,0},{1,129},{129,1},{2,130},{130,2},{3,131},{131,3},{4... | collective-permute-start | bytes 884744 | tf_op jit(solution)/shard_map/ppermute | solution.py:88
Sparse Core Ops, SparseCore 0:
  9.8 98.4 all-gather.1
